TPU v7x, 32 devices: a whole 2x2x4 slice. The times are simulated.
32 devices in a mesh: tok: 8 (over z, x), grp: 4 (over y, core).
Axes of the slice: x: 2, y: 2, z: 4, core: 2. Of those that a mesh axis runs over, the one named last changes fastest.
Arguments:
- queries: bfloat16 [1536, 2048], P('tok', 'grp'), may hold values from -72 to 72
- new_keys: bfloat16 [1536, 2048], P('tok', 'grp'), may hold values from -8 to 8
- new_values: bfloat16 [1536, 2048], P('tok', 'grp'), may hold values from -6 to 6
- residual: bfloat16 [1536, 2048], P('tok', 'grp'), may hold values from -6 to 6
- w_out: bfloat16 [2048, 2048], P('grp'), may hold values from -0.125 to 0.125
- leaf_keys: bfloat16 [8, 512, 2048], P('tok', None, 'grp'), may hold values from -6 to 6
- leaf_values: bfloat16 [8, 512, 2048], P('tok', None, 'grp'), may hold values from -6 to 6
- upper_keys: bfloat16 [6, 1024, 2048], P(None, 'tok', 'grp'), may hold values from -8 to 8
- upper_values: bfloat16 [6, 1024, 2048], P(None, 'tok', 'grp'), may hold values from -6 to 6
- req_len: int32 [8], replicated, may hold values from 48 to 192, as said below
- leaf_mid: int32 [8], replicated, may hold values from 0 to 3
- mid_root: int32 [4], replicated, may hold values from 0 to 1, as said below
- upper_len: int32 [6], replicated, may hold values from 256 to 1024, as said below
- leaf_len: int32 [8], replicated, may hold values from 128 to 512, as said below
Outputs:
- hidden_out: bfloat16 [1536, 2048], P('tok', 'grp')
Inputs may be any that keep to these rules, and one draw needn't show every extreme that they name: `req_len`: some request has exactly 192 new tokens. `mid_root`: each root is the parent of 2 mids. `upper_len`: the first 2 entries are roots and equal 1024. `leaf_len`: some leaf has exactly 512 positions.
All inputs are finite; a program needn't handle non-finite values.
Results may differ from a plain program's by a relative error of at most 0.008.
Values may be sent and summed in bfloat16 or wider, within the bound.
No kernel may reach another device: no remote copies, remote signals or barrier semaphores. Data moves between devices by JAX's collectives and lax.ppermute only.
A program may use at most 64 MiB of HBM per device.

v0:
```python
import jax
import jax.numpy as jnp
from jax import lax
from jax.sharding import PartitionSpec as P

HEAD_DIM = 128
NEG_FILL = -1e30


def partial_attention(query_rows, key_rows, values, allowed, head_count):
    head_width = query_rows.shape[1] // head_count
    parts = []
    for head in range(head_count):
        cols = slice(head * head_width, (head + 1) * head_width)
        scores = lax.dot_general(
            query_rows[:, cols],
            key_rows[:, cols],
            (((1,), (1,)), ((), ())),
            preferred_element_type=jnp.float32,
        ) * head_width ** (-0.5)
        scores = jnp.where(allowed, scores, NEG_FILL)
        row_max = jnp.max(scores, axis=1, keepdims=True)
        exp_scores = jnp.where(allowed, jnp.exp(scores - row_max), 0.0)
        row_total = jnp.sum(exp_scores, axis=1, keepdims=True)
        weighted = jnp.dot(
            exp_scores.astype(jnp.bfloat16), values[:, cols], preferred_element_type=jnp.float32
        )
        parts.append((row_max, row_total, weighted))
    return parts


def combine(earlier, latter):
    merged = []
    for (max_a, total_a, sum_a), (max_b, total_b, sum_b) in zip(earlier, latter):
        new_max = jnp.maximum(max_a, max_b)
        scale_a = jnp.exp(max_a - new_max)
        scale_b = jnp.exp(max_b - new_max)
        merged.append(
            (new_max, total_a * scale_a + total_b * scale_b, sum_a * scale_a + sum_b * scale_b)
        )
    return merged


def shards(
    queries,
    new_keys,
    new_values,
    residual,
    w_out,
    leaf_keys,
    leaf_values,
    upper_keys,
    upper_values,
    req_len,
    leaf_mid,
    mid_root,
    upper_len,
    leaf_len,
):
    dev_count = lax.axis_size("tok")
    my_index = lax.axis_index("tok")
    row_count = queries.shape[0]
    col_count = queries.shape[1]
    head_count = col_count // HEAD_DIM
    head_width = col_count // head_count
    mid_count = mid_root.shape[0]
    node_count = upper_len.shape[0]
    root_count = node_count - mid_count
    chunk = upper_keys.shape[1]
    owned = (jnp.arange(dev_count, dtype=jnp.int32) == my_index).astype(jnp.int32)
    my_length = jnp.sum(owned * req_len)
    my_mid = jnp.sum(owned * leaf_mid)
    my_leaf_len = jnp.sum(owned * leaf_len)
    my_root = jnp.sum((jnp.arange(mid_count) == my_mid).astype(jnp.int32) * mid_root)
    node_ids = jnp.arange(node_count)
    root_len = jnp.sum((node_ids == my_root).astype(jnp.int32) * upper_len)
    mid_len = jnp.sum((node_ids == root_count + my_mid).astype(jnp.int32) * upper_len)
    position = jnp.arange(row_count, dtype=jnp.int32)
    is_live = position < my_length
    leaf_count = leaf_keys.shape[1]
    local_keys = jnp.concatenate([leaf_keys[0], new_keys], axis=0)
    local_values = jnp.concatenate([leaf_values[0], new_values], axis=0)
    leaf_allowed = jnp.broadcast_to(
        (jnp.arange(leaf_count) < my_leaf_len)[None, :], (row_count, leaf_count)
    )
    new_allowed = (position[None, :] <= position[:, None]) & is_live[None, :]
    local_allowed = jnp.concatenate([leaf_allowed, new_allowed], axis=1)
    if dev_count * row_count * col_count * 4 <= 8 << 20:
        merged = query_plan(
            queries,
            local_keys,
            local_values,
            local_allowed,
            upper_keys,
            upper_values,
            leaf_mid,
            mid_root,
            upper_len,
            head_count,
            my_index,
            root_count,
            chunk,
        )
    else:
        merged = node_plan(
            queries,
            local_keys,
            local_values,
            local_allowed,
            upper_keys,
            upper_values,
            leaf_mid,
            mid_root,
            root_len,
            mid_len,
            head_count,
            root_count,
            chunk,
        )
    attended = jnp.concatenate([part[2] / part[1] for part in merged], axis=1)
    attention = jnp.where(is_live[:, None], attended, 0.0).astype(jnp.bfloat16)
    projected = jnp.dot(attention, w_out, preferred_element_type=jnp.float32)
    mixed = lax.psum_scatter(
        projected.astype(jnp.bfloat16), "grp", scatter_dimension=1, tiled=True
    ).astype(jnp.float32)
    return (residual.astype(jnp.float32) + mixed).astype(jnp.bfloat16)


def node_plan(
    queries,
    local_keys,
    local_values,
    local_allowed,
    upper_keys,
    upper_values,
    leaf_mid,
    mid_root,
    root_len,
    mid_len,
    head_count,
    root_count,
    chunk,
):
    dev_count = lax.axis_size("tok")
    col_count = queries.shape[1]
    dest_mid = leaf_mid.astype(jnp.int32)
    dest_root = jnp.take(mid_root, dest_mid).astype(jnp.int32)
    dest_nodes = jnp.stack([dest_root, root_count + dest_mid], axis=1)
    send = jnp.concatenate(
        [
            upper_keys.at[dest_nodes].get(mode="promise_in_bounds"),
            upper_values.at[dest_nodes].get(mode="promise_in_bounds"),
        ],
        axis=1,
    )
    received = lax.all_to_all(send, "tok", 0, 0, tiled=True)
    recv_keys = received[:, :2]
    recv_values = received[:, 2:]
    local_part = partial_attention(queries, local_keys, local_values, local_allowed, head_count)
    upper_pos = (
        jnp.arange(dev_count, dtype=jnp.int32)[:, None, None] * chunk
        + jnp.arange(chunk, dtype=jnp.int32)[None, None, :]
    )
    upper_limit = jnp.stack([root_len, mid_len])[None, :, None]
    upper_ok = (upper_pos < upper_limit).reshape(-1)
    upper_part = partial_attention(
        queries,
        recv_keys.reshape(-1, col_count),
        recv_values.reshape(-1, col_count),
        upper_ok[None, :],
        head_count,
    )
    return combine(local_part, upper_part)


def query_plan(
    queries,
    local_keys,
    local_values,
    local_allowed,
    upper_keys,
    upper_values,
    leaf_mid,
    mid_root,
    upper_len,
    head_count,
    my_index,
    root_count,
    chunk,
):
    dev_count = lax.axis_size("tok")
    row_count = queries.shape[0]
    col_count = queries.shape[1]
    head_width = col_count // head_count
    node_count = upper_keys.shape[0]
    scale = head_width ** (-0.5)
    all_queries = lax.all_gather(queries, "tok", axis=0, tiled=True)
    req_mid = leaf_mid.astype(jnp.int32)
    req_root = jnp.take(mid_root, req_mid).astype(jnp.int32)
    node_ids = jnp.arange(node_count, dtype=jnp.int32)
    node_used = (node_ids[None, :] == req_root[:, None]) | (
        node_ids[None, :] == root_count + req_mid[:, None]
    )
    pos_ok = (my_index * chunk + jnp.arange(chunk, dtype=jnp.int32))[None, :] < upper_len[:, None]
    seen = (node_used[:, :, None] & pos_ok[None, :, :]).reshape(dev_count, 1, node_count * chunk)
    flat_keys = upper_keys.reshape(node_count * chunk, col_count)
    flat_values = upper_values.reshape(node_count * chunk, col_count)
    upper_scores = []
    local_scores = []
    maxima = []
    for head in range(head_count):
        cols = slice(head * head_width, (head + 1) * head_width)
        scores = (
            lax.dot_general(
                all_queries[:, cols],
                flat_keys[:, cols],
                (((1,), (1,)), ((), ())),
                preferred_element_type=jnp.float32,
            )
            * scale
        )
        scores = jnp.where(seen, scores.reshape(dev_count, row_count, -1), NEG_FILL)
        upper_max = jnp.max(scores, axis=2)
        own = lax.dynamic_slice_in_dim(upper_max, my_index, 1, axis=0)
        mine = (
            lax.dot_general(
                queries[:, cols],
                local_keys[:, cols],
                (((1,), (1,)), ((), ())),
                preferred_element_type=jnp.float32,
            )
            * scale
        )
        mine = jnp.where(local_allowed, mine, NEG_FILL)
        own = jnp.maximum(own, jnp.max(mine, axis=1)[None, :])
        maxima.append(lax.dynamic_update_slice_in_dim(upper_max, own, my_index, axis=0))
        upper_scores.append(scores)
        local_scores.append(mine)
    row_max = lax.pmax(jnp.stack(maxima, axis=2), "tok")
    sums = []
    totals = []
    for head in range(head_count):
        cols = slice(head * head_width, (head + 1) * head_width)
        head_max = row_max[:, :, head : head + 1]
        exps = jnp.where(seen, jnp.exp(upper_scores[head] - head_max), 0.0)
        totals.append(jnp.sum(exps, axis=2))
        sums.append(
            jnp.dot(
                exps.reshape(dev_count * row_count, -1).astype(jnp.bfloat16),
                flat_values[:, cols],
                preferred_element_type=jnp.float32,
            )
        )
    upper_sum, upper_total = lax.psum_scatter(
        (
            jnp.concatenate(sums, axis=1),
            jnp.stack(totals, axis=2).reshape(dev_count * row_count, head_count),
        ),
        "tok",
        scatter_dimension=0,
        tiled=True,
    )
    own_max = lax.dynamic_index_in_dim(row_max, my_index, axis=0, keepdims=False)
    merged = []
    for head in range(head_count):
        cols = slice(head * head_width, (head + 1) * head_width)
        exps = jnp.where(
            local_allowed, jnp.exp(local_scores[head] - own_max[:, head : head + 1]), 0.0
        )
        total = jnp.sum(exps, axis=1, keepdims=True) + upper_total[:, head : head + 1]
        weighted = (
            jnp.dot(
                exps.astype(jnp.bfloat16), local_values[:, cols], preferred_element_type=jnp.float32
            )
            + upper_sum[:, cols]
        )
        merged.append((None, total, weighted))
    return merged


def solution(mesh):
    in_specs = (
        P("tok", "grp"),
        P("tok", "grp"),
        P("tok", "grp"),
        P("tok", "grp"),
        P("grp", None),
        P("tok", None, "grp"),
        P("tok", None, "grp"),
        P(None, "tok", "grp"),
        P(None, "tok", "grp"),
        P(),
        P(),
        P(),
        P(),
        P(),
    )
    out_specs = P("tok", "grp")
    return jax.shard_map(shards, mesh=mesh, in_specs=in_specs, out_specs=out_specs, check_vma=False)
```

profile of v0, /device:TPU:0, one launch (start us, length us, event | category | flops | bytes accessed | tf_op | source)
XLA Modules:
  0.0 299.4 jit_solution(17973138903810217957)
XLA Ops:
  15.2 2.0 fusion.134
  17.1 2.0 fusion.133
  19.2 2.0 fusion.132
  21.1 2.0 fusion.131
  23.1 33.2 %all-gather.2.cloned.1.call-done = bf16[1536,512]{1,0:T(8,128)(2,1)} async-done(((bf16[192,512]{1,0:T(8,128)(2,1)}), bf16[1536,512]{1,0:T(8,128)(2,1)}) %all-gather.2.cloned.1.call-update) | async-done | bytes 1572880 | tf_op jit(solution)/shard_map/all_gather | solution.py:197
  56.3 2.0 fusion.40
  61.9 4.7 %fusion = (f32[1536]{0:T(1024)S(1)}, f32[1536]{0:T(1024)S(1)}, f32[1536]{0:T(1024)S(1)}, f32[1536]{0:T(1024)S(1)}, f32[1536,768]{0,1:T(8,128)}) fusion(pred[1536,768]{0,1:T(32,128)(4,1)S(1)} %copy.27, f32[1536,768]{0,1:T(8,128)S(1)} %fusion.40, f32[1536,768]{0,1:T(8,128)S(1)} %fusion.42, f32[1536,768]{0,1:T(8,128)S(1)} %fusion.44, ...), kind=kOutput, calls=%fused_computation.9 | convolution fusion | flops 316139520 | bytes 20668416 | tf_op jit(solution)/shard_map/dot_general | solution.py:214
  67.4 35.0 %pmax.7 = f32[8,192,4]{1,0,2:T(8,128)S(1)} all-reduce(f32[8,192,4]{1,0,2:T(8,128)S(1)} %pad_maximum_fusion.5), channel_id=1, replica_groups=mesh['tok'=8,'grp'=4] {'tok'}, use_global_device_ids=true, to_apply=%region_10.11 | all-reduce | flops 6144 | bytes 49152 | tf_op jit(solution)/shard_map/pmax | solution.py:239
  102.7 4.9 %fusion.16 = f32[1536,128]{0,1:T(8,128)S(1)} fusion(pred[1536,768]{0,1:T(32,128)(4,1)} %copy-done.4, f32[1536,768]{0,1:T(8,128)} %copy-done.3, f32[1536]{0:T(1024)S(1)} %sub.94, bf16[768,512]{1,0:T(8,128)(2,1)} %bitcast.111), kind=kOutput, calls=%fused_computation.25 | convolution fusion | flops 307888128 | bytes 6887424 | tf_op jit(solution)/shard_map/dot_general | solution.py:248
  107.7 2.3 fusion.14
  110.0 5.4 %fusion.18 = f32[1536,128]{0,1:T(8,128)} fusion(pred[1536,768]{0,1:T(32,128)(4,1)S(1)} %copy-done.5, f32[1536,768]{0,1:T(8,128)} %get-tuple-element.31, f32[1536]{0:T(1024)S(1)} %sub.91, bf16[768,512]{1,0:T(8,128)(2,1)S(1)} %bitcast.113), kind=kOutput, calls=%fused_computation.26 | convolution fusion | flops 307888128 | bytes 6889472 | tf_op jit(solution)/shard_map/dot_general | solution.py:248
  115.5 4.7 %fusion.4 = (f32[1536]{0:T(1024)S(1)}, f32[1536]{0:T(1024)S(1)}, f32[1536]{0:T(1024)S(1)}, f32[1536]{0:T(1024)S(1)}) fusion(pred[1536,768]{0,1:T(32,128)(4,1)S(1)} %copy-done.5, f32[1536,768]{0,1:T(8,128)S(1)} %bitcast.80, f32[1536]{0:T(1024)S(1)} %sub.91, f32[1536]{0:T(1024)S(1)} %sub.100, f32[1536,768]{0,1:T(8,128)S(1)} %bitcast.74, f32[1536]{0:T(1024)S(1)} %sub.97, ...), kind=kLoop, calls=%fused_computation.14 | loop fusion | flops 23586816 | bytes 20103168 | tf_op jit(solution)/shard_map/reduce_sum | solution.py:246
  120.2 2.3 fusion.12
  123.9 3.5 %pad_maximum_fusion = f32[1536,512]{0,1:T(8,128)} fusion(f32[1536,128]{0,1:T(8,128)} %fusion.12, f32[1536,128]{0,1:T(8,128)} %fusion.14, f32[1536,128]{0,1:T(8,128)S(1)} %fusion.16, f32[1536,128]{0,1:T(8,128)} %fusion.18), kind=kLoop, calls=%fused_computation.13 | loop fusion | flops 2359296 | bytes 6291456 | tf_op jit(solution)/shard_map/concatenate | solution.py:256
  127.4 3.7 %copy.43 = f32[1536,512]{1,0:T(8,128)} copy(f32[1536,512]{0,1:T(8,128)} %pad_maximum_fusion) | data formatting | bytes 6291456
  131.3 2.0 fusion.32
  133.3 50.3 %reduce-scatter.12.cloned.1.call-done = f32[192,4]{1,0:T(8,128)} async-done(((f32[1536,4]{1,0:T(8,128)}), f32[192,4]{1,0:T(8,128)}) %reduce-scatter.12.cloned.1.call-update) | async-done | bytes 3088
  183.6 1.8 fusion.128
  187.6 73.3 %reduce-scatter.10.cloned.1.call-done = f32[192,512]{1,0:T(8,128)} async-done(((f32[1536,512]{1,0:T(8,128)}), f32[192,512]{1,0:T(8,128)}) %reduce-scatter.10.cloned.1.call-update) | async-done | bytes 393232 | tf_op jit(solution)/shard_map/reduce_scatter | solution.py:254
  260.9 1.5 fusion.28
  262.4 1.5 fusion.29
  266.5 2.1 convolution_convert_fusion
  268.6 22.5 %reduce-scatter.8.cloned.1.call-done = bf16[192,512]{1,0:T(8,128)(2,1)} async-done(((bf16[192,2048]{1,0:T(8,128)(2,1)}), bf16[192,512]{1,0:T(8,128)(2,1)}) %reduce-scatter.8.cloned.1.call-update) | async-done | bytes 196624 | tf_op jit(solution)/shard_map/reduce_scatter | solution.py:123
  291.2 1.7 add_convert_fusion
  (129 shorter events, 19.3 us)
Async XLA Ops:
  6.5 260.0 %copy-start = (bf16[512,2048]{1,0:T(8,128)(2,1)S(1)}, bf16[512,2048]{1,0:T(8,128)(2,1)}, u32[]{:S(2)}) copy-start(bf16[512,2048]{1,0:T(8,128)(2,1)} %param.18) | copy-start | bytes 6291460
  6.5 10.6 %copy-start.7 = (bf16[192,512]{1,0:T(8,128)(2,1)S(1)}, bf16[192,512]{1,0:T(8,128)(2,1)}, u32[]{:S(2)}) copy-start(bf16[192,512]{1,0:T(8,128)(2,1)} %param.15) | copy-start | bytes 589828
  6.5 49.8 %all-gather.2.cloned.1.call-start = ((), (), s32[]{:S(2)}) async-start(), calls=%async_computation.3 | async-start | bytes 1769472 | tf_op jit(solution)/shard_map/all_gather | solution.py:197
  7.3 176.3 %reduce-scatter.12.cloned.1.call-start = ((), (), s32[]{:S(2)}) async-start(), calls=%async_computation.6 | async-start | bytes 884736
  12.4 47.5 %copy-start.4 = (pred[1536,768]{0,1:T(32,128)(4,1)}, pred[1536,768]{0,1:T(32,128)(4,1)S(1)}, u32[]{:S(2)}) copy-start(pred[1536,768]{0,1:T(32,128)(4,1)S(1)} %copy.27) | copy-start | bytes 3538948
  15.1 4.0 %copy-start.17 = (pred[192]{0:T(512)(128)(4,1)}, pred[192]{0:T(512)(128)(4,1)S(1)}, u32[]{:S(2)}) copy-start(pred[192]{0:T(512)(128)(4,1)S(1)} %iota_compare_fusion.4) | copy-start | bytes 580
  61.9 4.7 %copy-start.3 = (f32[1536,768]{0,1:T(8,128)}, f32[1536,768]{0,1:T(8,128)S(1)}, u32[]{:S(2)}) copy-start(f32[1536,768]{0,1:T(8,128)S(1)} %fusion.44) | copy-start | bytes 14155780
  102.4 5.2 %slice-start.2 = ((s8[4718592]{0:T(1024)(128)(4,1)}), s8[524288]{0:T(1024)(128)(4,1)S(1)}, s32[]{:S(2)}) async-start(s8[4718592]{0:T(1024)(128)(4,1)} %bitcast.75), calls=%async_computation.9 | async-start | bytes 1048576
  102.7 5.0 %slice-start.3 = ((s8[4718592]{0:T(1024)(128)(4,1)}), s8[4194304]{0:T(1024)(128)(4,1)S(1)}, s32[]{:S(2)}) async-start(s8[4718592]{0:T(1024)(128)(4,1)} %bitcast.75), calls=%async_computation.10 | async-start | bytes 8388608
  102.7 5.0 %copy-start.5 = (pred[1536,768]{0,1:T(32,128)(4,1)S(1)}, pred[1536,768]{0,1:T(32,128)(4,1)}, u32[]{:S(2)}) copy-start(pred[1536,768]{0,1:T(32,128)(4,1)} %copy-done.4) | copy-start | bytes 3538948
  102.7 5.0 %copy-start.18 = (bf16[6,128,512]{2,1,0:T(8,128)(2,1)S(1)}, bf16[6,128,512]{2,1,0:T(8,128)(2,1)}, u32[]{:S(2)}) copy-start(bf16[6,128,512]{2,1,0:T(8,128)(2,1)} %param.22) | copy-start | bytes 2359300
  107.7 7.8 %slice-start = ((s8[4718592]{0:T(1024)(128)(4,1)}), s8[4194304]{0:T(1024)(128)(4,1)S(1)}, s32[]{:S(2)}) async-start(s8[4718592]{0:T(1024)(128)(4,1)} %bitcast.73), calls=%async_computation.7 | async-start | bytes 8388608
  107.7 7.8 %slice-start.4 = ((s8[4718592]{0:T(1024)(128)(4,1)}), s8[4194304]{0:T(1024)(128)(4,1)S(1)}, s32[]{:S(2)}) async-start(s8[4718592]{0:T(1024)(128)(4,1)} %bitcast.77), calls=%async_computation.11 | async-start | bytes 8388608
  107.7 7.8 %slice-start.6 = ((s8[4718592]{0:T(1024)(128)(4,1)}), s8[4194304]{0:T(1024)(128)(4,1)S(1)}, s32[]{:S(2)}) async-start(s8[4718592]{0:T(1024)(128)(4,1)} %bitcast.79), calls=%async_computation.13 | async-start | bytes 8388608
  110.0 5.4 %slice-start.1 = ((s8[4718592]{0:T(1024)(128)(4,1)}), s8[524288]{0:T(1024)(128)(4,1)S(1)}, s32[]{:S(2)}) async-start(s8[4718592]{0:T(1024)(128)(4,1)} %bitcast.73), calls=%async_computation.8 | async-start | bytes 1048576
  110.0 5.5 %slice-start.5 = ((s8[4718592]{0:T(1024)(128)(4,1)}), s8[524288]{0:T(1024)(128)(4,1)S(1)}, s32[]{:S(2)}) async-start(s8[4718592]{0:T(1024)(128)(4,1)} %bitcast.77), calls=%async_computation.12 | async-start | bytes 1048576
  110.0 5.5 %slice-start.7 = ((s8[4718592]{0:T(1024)(128)(4,1)}), s8[524288]{0:T(1024)(128)(4,1)S(1)}, s32[]{:S(2)}) async-start(s8[4718592]{0:T(1024)(128)(4,1)} %bitcast.79), calls=%async_computation.14 | async-start | bytes 1048576
  123.8 137.0 %reduce-scatter.10.cloned.1.call-start = ((), (), s32[]{:S(2)}) async-start(), calls=%async_computation.5 | async-start | bytes 3538944 | tf_op jit(solution)/shard_map/reduce_scatter | solution.py:254
  127.4 3.9 %copy-start.9 = (f32[192,704]{1,0:T(8,128)S(1)}, f32[192,704]{1,0:T(8,128)}, u32[]{:S(2)}) copy-start(f32[192,704]{1,0:T(8,128)} %get-tuple-element.35) | copy-start | bytes 1622020
  131.1 160.1 %reduce-scatter.8.cloned.1.call-start = ((), (), s32[]{:S(2)}) async-start(), calls=%async_computation.4 | async-start | bytes 983040 | tf_op jit(solution)/shard_map/reduce_scatter | solution.py:123
  187.5 77.7 %copy-start.13 = (f32[192,1]{0,1:T(1,128)S(1)}, f32[192,1]{0,1:T(1,128)}, u32[]{:S(2)}) copy-start(f32[192,1]{0,1:T(1,128)} %copy-done.12) | copy-start | bytes 2308
  260.8 4.4 %copy-start.19 = (bf16[1,512,512]{2,1,0:T(8,128)(2,1)S(1)}, bf16[1,512,512]{2,1,0:T(8,128)(2,1)}, u32[]{:S(2)}) copy-start(bf16[1,512,512]{2,1,0:T(8,128)(2,1)} %param.20) | copy-start | bytes 1572868
  260.9 4.4 %copy-start.20 = (bf16[192,512]{1,0:T(8,128)(2,1)S(1)}, bf16[192,512]{1,0:T(8,128)(2,1)}, u32[]{:S(2)}) copy-start(bf16[192,512]{1,0:T(8,128)(2,1)} %param.16) | copy-start | bytes 589828
  262.4 28.8 %copy-start.11 = (bf16[192,512]{1,0:T(8,128)(2,1)S(1)}, bf16[192,512]{1,0:T(8,128)(2,1)}, u32[]{:S(2)}) copy-start(bf16[192,512]{1,0:T(8,128)(2,1)} %param.17) | copy-start | bytes 589828
  (9 other events, 20.8 us)
Sparse Core Ops, SparseCore 0:
  9.5 46.7 all-gather.1
  123.9 59.5 reduce-scatter.11
  187.6 73.2 reduce-scatter.9
  268.8 22.3 reduce-scatter.7
where the time goes:
time: 300 us; the launch traced here: 299 us
  waiting for transfers between devices  180 us (60%)
  matrix products  38.8 us (13%)
  blocking collectives  35 us (12%)
  other arithmetic  16 us (5%)
  local copies, waits for them, and re-layouts  15.6 us (5%)
  between operations  13.7 us (5%)
    reduce_scatter x1, waiting for transfers between devices, query_plan(): lax.psum_scatter((jnp.concatenate(sums, axis=1), jnp.stack(totals, axis=2...  73.3 us
    unnamed x5, waiting for transfers between devices  51.1 us
    pmax x1, blocking collectives, query_plan(): row_max = lax.pmax(jnp.stack(maxima, axis=2), 'tok')  35 us
    all_gather x1, waiting for transfers between devices, query_plan(): all_queries = lax.all_gather(queries, 'tok', axis=0, tiled=True)  33.2 us
    reduce_scatter x1, waiting for transfers between devices, shards(): lax.psum_scatter(projected.astype(jnp.bfloat16), 'grp', scatter_dimension...  22.5 us
    dot_general x4, matrix products, query_plan(): jnp.dot(exps.reshape(dev_count * row_count, -1).astype(jnp.bfloat16), fla...  15 us
    unnamed x65, local copies, waits for them, and re-layouts  9.09 us
    dot_general x4, matrix products, query_plan(): lax.dot_general(all_queries[:, cols], flat_keys[:, cols], (((1,), (1,)),...  8.22 us
  transfers between devices with their start and end apart: 4, of which 4 were waited for; matrix products, arithmetic and copies ran while one was open for 10% of the time, Pallas kernels for 0%

commit v1 on v0

--- a/solution.py
+++ b/solution.py
@@ -194,7 +194,9 @@
     head_width = col_count // head_count
     node_count = upper_keys.shape[0]
     scale = head_width ** (-0.5)
-    all_queries = lax.all_gather(queries, "tok", axis=0, tiled=True)
+    all_queries = jnp.concatenate(
+        lax.all_to_all(jnp.stack([queries] * lax.axis_size("tok")), "tok", 0, 0), axis=0
+    )
     req_mid = leaf_mid.astype(jnp.int32)
     req_root = jnp.take(mid_root, req_mid).astype(jnp.int32)
     node_ids = jnp.arange(node_count, dtype=jnp.int32)

time: 300 us -> 299 us (level)
  waiting for transfers between devices: 180 us -> 171 us
  starting transfers between devices: 0.12 us -> 7.37 us
  matrix products: 38.8 us -> 42.3 us
    all_gather x1 -> x0, waiting for transfers between devices: 33.2 us -> none  [query_plan(): all_queries = lax.all_gather(queries, 'tok', axis=0, tiled=True)]
    all_to_all x0 -> x1, waiting for transfers between devices: none -> 24.4 us  [query_plan(): lax.all_to_all(jnp.stack([queries] * lax.axis_size('tok')), 'tok', 0, 0)]
    all_to_all x0 -> x1, starting transfers between devices: none -> 7.25 us  [query_plan(): lax.all_to_all(jnp.stack([queries] * lax.axis_size('tok')), 'tok', 0, 0)]
    dot_general x4, matrix products: 8.22 us -> 11.6 us  [query_plan(): lax.dot_general(all_queries[:, cols], flat_keys[:, cols], (((1,), (1,)),...]
    unnamed x65 -> x73, local copies, waits for them, and re-layouts: 9.09 us -> 7.19 us
    unnamed x5 -> x4, waiting for transfers between devices: 51.1 us -> 50.5 us
  transfers between devices with their start and end apart: 4 -> 4, of which waited for: 4 -> 4; matrix products, arithmetic and copies ran while one was open for 10% -> 9% of each run, Pallas kernels for 0% -> 0%
where the time goes in v1:
time: 299 us
  waiting for transfers between devices  171 us (57%)
  matrix products  42.3 us (14%)
  blocking collectives  35.3 us (12%)
  local copies, waits for them, and re-layouts  14.8 us (5%)
  other arithmetic  14.1 us (5%)
  between operations  13.8 us (5%)
  starting transfers between devices  7.37 us (2%)
    reduce_scatter x1, waiting for transfers between devices, query_plan(): lax.psum_scatter((jnp.concatenate(sums, axis=1), jnp.stack(totals, axis=2...  73.5 us
    unnamed x4, waiting for transfers between devices  50.5 us
    pmax x1, blocking collectives, query_plan(): row_max = lax.pmax(jnp.stack(maxima, axis=2), 'tok')  35.3 us
    all_to_all x1, waiting for transfers between devices, query_plan(): lax.all_to_all(jnp.stack([queries] * lax.axis_size('tok')), 'tok', 0, 0)  24.4 us
    reduce_scatter x1, waiting for transfers between devices, shards(): lax.psum_scatter(projected.astype(jnp.bfloat16), 'grp', scatter_dimension...  22.5 us
    dot_general x4, matrix products, query_plan(): jnp.dot(exps.reshape(dev_count * row_count, -1).astype(jnp.bfloat16), fla...  15 us
    dot_general x4, matrix products, query_plan(): lax.dot_general(all_queries[:, cols], flat_keys[:, cols], (((1,), (1,)),...  11.6 us
    dot_general x4, matrix products, query_plan(): lax.dot_general(queries[:, cols], local_keys[:, cols], (((1,), (1,)), (()...  7.98 us
  transfers between devices with their start and end apart: 4, of which 4 were waited for; matrix products, arithmetic and copies ran while one was open for 9% of the time, Pallas kernels for 0%

profile of v1, /device:TPU:0, one launch (start us, length us, event | category | flops | bytes accessed | tf_op | source)
XLA Modules:
  0.0 298.6 jit_solution(11753949757705351355)
XLA Ops:
  6.6 2.4 stack.49
  8.9 7.3 %all-to-all-start = ((bf16[8,192,512]{2,1,0:T(8,128)(2,1)}), bf16[8,192,512]{2,1,0:T(8,128)(2,1)}, u32[]{:S(2)}, u32[]{:S(2)}) async-start(bf16[8,192,512]{2,1,0:T(8,128)(2,1)} %stack.49), calls=%async_computation | async-start | bytes 3145728 | tf_op jit(solution)/shard_map/all_to_all | solution.py:198
  20.9 2.0 fusion.134
  23.0 2.0 fusion.133
  25.0 2.0 fusion.132
  26.9 2.0 fusion.131
  28.9 24.4 %all-to-all-done = bf16[8,192,512]{2,1,0:T(8,128)(2,1)} async-done(((bf16[8,192,512]{2,1,0:T(8,128)(2,1)}), bf16[8,192,512]{2,1,0:T(8,128)(2,1)}, u32[]{:S(2)}, u32[]{:S(2)}) %all-to-all-start) | async-done | bytes 1572896 | tf_op jit(solution)/shard_map/all_to_all | solution.py:198
  53.3 1.9 fusion.40
  55.2 2.1 fusion.42
  57.3 2.1 fusion.44
  59.4 5.6 %fusion = (f32[1536]{0:T(1024)S(1)}, f32[1536]{0:T(1024)S(1)}, f32[1536]{0:T(1024)S(1)}, f32[1536]{0:T(1024)S(1)}, f32[1536,768]{0,1:T(8,128)}) fusion(pred[1536,768]{0,1:T(32,128)(4,1)S(1)} %copy.27, f32[1536,768]{0,1:T(8,128)S(1)} %fusion.40, f32[1536,768]{0,1:T(8,128)S(1)} %fusion.42, f32[1536,768]{0,1:T(8,128)S(1)} %fusion.44, ...), kind=kOutput, calls=%fused_computation.9 | convolution fusion | flops 316139520 | bytes 20668416 | tf_op jit(solution)/shard_map/dot_general | solution.py:216
  65.8 35.3 %pmax.7 = f32[8,192,4]{1,0,2:T(8,128)S(1)} all-reduce(f32[8,192,4]{1,0,2:T(8,128)S(1)} %pad_maximum_fusion.5), channel_id=1, replica_groups=mesh['tok'=8,'grp'=4] {'tok'}, use_global_device_ids=true, to_apply=%region_10.11 | all-reduce | flops 6144 | bytes 49152 | tf_op jit(solution)/shard_map/pmax | solution.py:241
  101.4 4.9 %fusion.16 = f32[1536,128]{0,1:T(8,128)S(1)} fusion(pred[1536,768]{0,1:T(32,128)(4,1)} %copy-done.5, f32[1536,768]{0,1:T(8,128)} %copy-done.4, f32[1536]{0:T(1024)S(1)} %sub.94, bf16[768,512]{1,0:T(8,128)(2,1)} %bitcast.112), kind=kOutput, calls=%fused_computation.25 | convolution fusion | flops 307888128 | bytes 6887424 | tf_op jit(solution)/shard_map/dot_general | solution.py:250
  106.4 2.3 fusion.14
  108.8 5.4 %fusion.18 = f32[1536,128]{0,1:T(8,128)} fusion(pred[1536,768]{0,1:T(32,128)(4,1)S(1)} %copy-done.6, f32[1536,768]{0,1:T(8,128)} %get-tuple-element.31, f32[1536]{0:T(1024)S(1)} %sub.91, bf16[768,512]{1,0:T(8,128)(2,1)S(1)} %bitcast.114), kind=kOutput, calls=%fused_computation.26 | convolution fusion | flops 307888128 | bytes 6889472 | tf_op jit(solution)/shard_map/dot_general | solution.py:250
  114.2 4.7 %fusion.4 = (f32[1536]{0:T(1024)S(1)}, f32[1536]{0:T(1024)S(1)}, f32[1536]{0:T(1024)S(1)}, f32[1536]{0:T(1024)S(1)}) fusion(pred[1536,768]{0,1:T(32,128)(4,1)S(1)} %copy-done.6, f32[1536,768]{0,1:T(8,128)S(1)} %bitcast.81, f32[1536]{0:T(1024)S(1)} %sub.91, f32[1536]{0:T(1024)S(1)} %sub.100, f32[1536,768]{0,1:T(8,128)S(1)} %bitcast.75, f32[1536]{0:T(1024)S(1)} %sub.97, ...), kind=kLoop, calls=%fused_computation.14 | loop fusion | flops 23586816 | bytes 20103168 | tf_op jit(solution)/shard_map/reduce_sum | solution.py:248
  118.9 2.3 fusion.12
  122.6 3.5 %pad_maximum_fusion = f32[1536,512]{0,1:T(8,128)} fusion(f32[1536,128]{0,1:T(8,128)} %fusion.12, f32[1536,128]{0,1:T(8,128)} %fusion.14, f32[1536,128]{0,1:T(8,128)S(1)} %fusion.16, f32[1536,128]{0,1:T(8,128)} %fusion.18), kind=kLoop, calls=%fused_computation.13 | loop fusion | flops 2359296 | bytes 6291456 | tf_op jit(solution)/shard_map/concatenate | solution.py:258
  126.1 3.7 %copy.43 = f32[1536,512]{1,0:T(8,128)} copy(f32[1536,512]{0,1:T(8,128)} %pad_maximum_fusion) | data formatting | bytes 6291456
  130.0 2.0 fusion.32
  132.0 50.5 %reduce-scatter.12.cloned.1.call-done = f32[192,4]{1,0:T(8,128)} async-done(((f32[1536,4]{1,0:T(8,128)}), f32[192,4]{1,0:T(8,128)}) %reduce-scatter.12.cloned.1.call-update) | async-done | bytes 3088
  186.5 73.5 %reduce-scatter.10.cloned.1.call-done = f32[192,512]{1,0:T(8,128)} async-done(((f32[1536,512]{1,0:T(8,128)}), f32[192,512]{1,0:T(8,128)}) %reduce-scatter.10.cloned.1.call-update) | async-done | bytes 393232 | tf_op jit(solution)/shard_map/reduce_scatter | solution.py:256
  265.7 2.2 convolution_convert_fusion
  267.9 22.5 %reduce-scatter.8.cloned.1.call-done = bf16[192,512]{1,0:T(8,128)(2,1)} async-done(((bf16[192,2048]{1,0:T(8,128)(2,1)}), bf16[192,512]{1,0:T(8,128)(2,1)}) %reduce-scatter.8.cloned.1.call-update) | async-done | bytes 196624 | tf_op jit(solution)/shard_map/reduce_scatter | solution.py:123
  (137 shorter events, 18.4 us)
Async XLA Ops:
  6.5 259.1 %copy-start = (bf16[512,2048]{1,0:T(8,128)(2,1)S(1)}, bf16[512,2048]{1,0:T(8,128)(2,1)}, u32[]{:S(2)}) copy-start(bf16[512,2048]{1,0:T(8,128)(2,1)} %param.18) | copy-start | bytes 6291460
  6.5 9.7 %copy-start.21 = (s32[8]{0:T(128)S(1)}, s32[8]{0:T(128)}, u32[]{:S(2)}) copy-start(s32[8]{0:T(128)} %param.24) | copy-start | bytes 100
  6.5 9.7 %copy-start.1 = (s32[4]{0:T(128)S(1)}, s32[4]{0:T(128)}, u32[]{:S(2)}) copy-start(s32[4]{0:T(128)} %param.25) | copy-start | bytes 52
  6.5 10.4 %copy-start.18 = (s32[6]{0:T(128)S(1)}, s32[6]{0:T(128)}, u32[]{:S(2)}) copy-start(s32[6]{0:T(128)} %param.26) | copy-start | bytes 76
  6.5 12.2 %copy-start.19 = (s32[8]{0:T(128)S(1)}, s32[8]{0:T(128)}, u32[]{:S(2)}) copy-start(s32[8]{0:T(128)} %param.23) | copy-start | bytes 100
  6.5 12.2 %copy-start.20 = (s32[8]{0:T(128)S(1)}, s32[8]{0:T(128)}, u32[]{:S(2)}) copy-start(s32[8]{0:T(128)} %param.27) | copy-start | bytes 100
  6.6 14.4 %copy-start.7 = (bf16[192,512]{1,0:T(8,128)(2,1)S(1)}, bf16[192,512]{1,0:T(8,128)(2,1)}, u32[]{:S(2)}) copy-start(bf16[192,512]{1,0:T(8,128)(2,1)} %param.15) | copy-start | bytes 589828
  8.9 44.4 %all-to-all-start = ((bf16[8,192,512]{2,1,0:T(8,128)(2,1)}), bf16[8,192,512]{2,1,0:T(8,128)(2,1)}, u32[]{:S(2)}, u32[]{:S(2)}) async-start(bf16[8,192,512]{2,1,0:T(8,128)(2,1)} %stack.49), calls=%async_computation | async-start | bytes 3145728 | tf_op jit(solution)/shard_map/all_to_all | solution.py:198
  16.2 166.3 %reduce-scatter.12.cloned.1.call-start = ((), (), s32[]{:S(2)}) async-start(), calls=%async_computation.6 | async-start | bytes 884736
  18.8 40.6 %copy-start.5 = (pred[1536,768]{0,1:T(32,128)(4,1)}, pred[1536,768]{0,1:T(32,128)(4,1)S(1)}, u32[]{:S(2)}) copy-start(pred[1536,768]{0,1:T(32,128)(4,1)S(1)} %copy.27) | copy-start | bytes 3538948
  59.4 5.6 %copy-start.4 = (f32[1536,768]{0,1:T(8,128)}, f32[1536,768]{0,1:T(8,128)S(1)}, u32[]{:S(2)}) copy-start(f32[1536,768]{0,1:T(8,128)S(1)} %fusion.44) | copy-start | bytes 14155780
  101.1 5.2 %slice-start.2 = ((s8[4718592]{0:T(1024)(128)(4,1)}), s8[524288]{0:T(1024)(128)(4,1)S(1)}, s32[]{:S(2)}) async-start(s8[4718592]{0:T(1024)(128)(4,1)} %bitcast.76), calls=%async_computation.9 | async-start | bytes 1048576
  101.4 5.0 %copy-start.6 = (pred[1536,768]{0,1:T(32,128)(4,1)S(1)}, pred[1536,768]{0,1:T(32,128)(4,1)}, u32[]{:S(2)}) copy-start(pred[1536,768]{0,1:T(32,128)(4,1)} %copy-done.5) | copy-start | bytes 3538948
  101.4 5.0 %copy-start.22 = (bf16[6,128,512]{2,1,0:T(8,128)(2,1)S(1)}, bf16[6,128,512]{2,1,0:T(8,128)(2,1)}, u32[]{:S(2)}) copy-start(bf16[6,128,512]{2,1,0:T(8,128)(2,1)} %param.22) | copy-start | bytes 2359300
  106.4 7.8 %slice-start = ((s8[4718592]{0:T(1024)(128)(4,1)}), s8[4194304]{0:T(1024)(128)(4,1)S(1)}, s32[]{:S(2)}) async-start(s8[4718592]{0:T(1024)(128)(4,1)} %bitcast.74), calls=%async_computation.7 | async-start | bytes 8388608
  106.4 7.8 %slice-start.4 = ((s8[4718592]{0:T(1024)(128)(4,1)}), s8[4194304]{0:T(1024)(128)(4,1)S(1)}, s32[]{:S(2)}) async-start(s8[4718592]{0:T(1024)(128)(4,1)} %bitcast.78), calls=%async_computation.11 | async-start | bytes 8388608
  106.4 7.8 %slice-start.6 = ((s8[4718592]{0:T(1024)(128)(4,1)}), s8[4194304]{0:T(1024)(128)(4,1)S(1)}, s32[]{:S(2)}) async-start(s8[4718592]{0:T(1024)(128)(4,1)} %bitcast.80), calls=%async_computation.13 | async-start | bytes 8388608
  108.7 5.4 %slice-start.1 = ((s8[4718592]{0:T(1024)(128)(4,1)}), s8[524288]{0:T(1024)(128)(4,1)S(1)}, s32[]{:S(2)}) async-start(s8[4718592]{0:T(1024)(128)(4,1)} %bitcast.74), calls=%async_computation.8 | async-start | bytes 1048576
  108.7 5.5 %slice-start.5 = ((s8[4718592]{0:T(1024)(128)(4,1)}), s8[524288]{0:T(1024)(128)(4,1)S(1)}, s32[]{:S(2)}) async-start(s8[4718592]{0:T(1024)(128)(4,1)} %bitcast.78), calls=%async_computation.12 | async-start | bytes 1048576
  108.7 5.5 %slice-start.7 = ((s8[4718592]{0:T(1024)(128)(4,1)}), s8[524288]{0:T(1024)(128)(4,1)S(1)}, s32[]{:S(2)}) async-start(s8[4718592]{0:T(1024)(128)(4,1)} %bitcast.80), calls=%async_computation.14 | async-start | bytes 1048576
  122.5 137.5 %reduce-scatter.10.cloned.1.call-start = ((), (), s32[]{:S(2)}) async-start(), calls=%async_computation.5 | async-start | bytes 3538944 | tf_op jit(solution)/shard_map/reduce_scatter | solution.py:256
  129.8 160.6 %reduce-scatter.8.cloned.1.call-start = ((), (), s32[]{:S(2)}) async-start(), calls=%async_computation.4 | async-start | bytes 983040 | tf_op jit(solution)/shard_map/reduce_scatter | solution.py:123
  186.4 78.0 %copy-start.13 = (f32[192,1]{0,1:T(1,128)S(1)}, f32[192,1]{0,1:T(1,128)}, u32[]{:S(2)}) copy-start(f32[192,1]{0,1:T(1,128)} %copy-done.12) | copy-start | bytes 2308
  261.5 28.8 %copy-start.11 = (bf16[192,512]{1,0:T(8,128)(2,1)S(1)}, bf16[192,512]{1,0:T(8,128)(2,1)}, u32[]{:S(2)}) copy-start(bf16[192,512]{1,0:T(8,128)(2,1)} %param.17) | copy-start | bytes 589828
  (13 other events, 41.8 us)
Sparse Core Ops, SparseCore 0:
  122.7 59.7 reduce-scatter.11
  186.5 73.4 reduce-scatter.9
  268.0 22.3 reduce-scatter.7
